TPU v7x, 32 devices: a whole 2x2x4 slice. The times are simulated.
32 devices in a mesh: dp: 8 (over z, y), tensor: 4 (over x, core).
Axes of the slice: x: 2, y: 2, z: 4, core: 2. Of those that a mesh axis runs over, the one named last changes fastest.
Arguments:
- query: bfloat16 [384, 8192], P('dp', 'tensor'), may hold values from -128 to 128
- new_key: bfloat16 [384, 512], P('dp', 'tensor'), may hold values from -6 to 6
- new_value: bfloat16 [384, 512], P('dp', 'tensor'), may hold values from -6 to 6
- cache_key: bfloat16 [384, 128, 512], P('dp', None, 'tensor'), may hold values from -6 to 6
- cache_value: bfloat16 [384, 128, 512], P('dp', None, 'tensor'), may hold values from -6 to 6
- lengths: int32 [384], P('dp'), may hold values from 1 to 128, as said below
- hidden_in: bfloat16 [384, 4096], P(('dp', 'tensor')), may hold values from -60 to 60
- out_weight: bfloat16 [8192, 4096], P('tensor', 'dp'), may hold values from -0.0625 to 0.0625
- norm_gain: float32 [4096], replicated, may hold values from 0.25 to 1.75
- route_ids: int32 [384, 8], P(('dp', 'tensor')), may hold values from 0 to 31, all different within a row; in each aligned block of 12 rows (0 to 11, 12 to 23, ...) at most 9 rows name the same one
- route_weight: float32 [384, 8], P(('dp', 'tensor')), may hold values from 0.03 to 0.3
- w_gate: bfloat16 [32, 4096, 768], P(('dp', 'tensor')), may hold values from -0.09375 to 0.09375
- w_up: bfloat16 [32, 4096, 768], P(('dp', 'tensor')), may hold values from -0.09375 to 0.09375
- w_down: bfloat16 [32, 768, 4096], P(('dp', 'tensor')), may hold values from -0.21875 to 0.21875
Outputs:
- attended: bfloat16 [384, 4096], P(('dp', 'tensor'))
- expert_mix: bfloat16 [384, 4096], P(('dp', 'tensor'))
Inputs may be any that keep to these rules, and one draw needn't show every extreme that they name: `lengths`: row 0 holds 128 positions. `route_ids`: A row names 8 different experts. In each aligned block of 12 rows (the rows of one device along dp+tensor) no expert is named by more than 9 rows, a bound that some block reaches.
All inputs are finite; a program needn't handle non-finite values.
Results may differ from a plain program's by a relative error of at most 0.013.
Values may be sent and summed in bfloat16 or wider, within the bound.
No kernel may reach another device: no remote copies, remote signals or barrier semaphores. Data moves between devices by JAX's collectives and lax.ppermute only.
A program may use at most 128 MiB of HBM per device.

v0:
```python
import math
import jax
import jax.numpy as jnp
from jax import lax
from jax.sharding import PartitionSpec as P

HD = 128


def attend_local(query, new_key, new_value, cache_key, cache_value, lengths):
    row_count = query.shape[0]
    cache_len = cache_key.shape[1]
    kv_here = new_key.shape[1] // HD
    grouping = query.shape[1] // (kv_here * HD)
    queries = query.reshape(row_count, kv_here, grouping, HD)
    cache_keys = cache_key.reshape(row_count, cache_len, kv_here, HD)
    values = cache_value.reshape(row_count, cache_len, kv_here, HD)
    own_key = new_key.reshape(row_count, kv_here, HD)
    own_value = new_value.reshape(row_count, kv_here, HD)
    factor = 1.0 / math.sqrt(HD)
    scores = (
        jnp.einsum("rkgd,rckd->rkgc", queries, cache_keys, preferred_element_type=jnp.float32)
        * factor
    )
    own_score = (
        jnp.einsum("rkgd,rkd->rkg", queries, own_key, preferred_element_type=jnp.float32) * factor
    )
    visible = (jnp.arange(cache_len, dtype=jnp.int32)[None, :] < lengths[:, None])[:, None, None, :]
    highest = jnp.maximum(jnp.max(jnp.where(visible, scores, -1e30), axis=-1), own_score)
    exponent = jnp.where(visible, jnp.exp(scores - highest[..., None]), 0.0)
    own_exponent = jnp.exp(own_score - highest)
    totals = jnp.sum(exponent, axis=-1) + own_exponent
    probability = (exponent / totals[..., None]).astype(jnp.bfloat16)
    own_probability = (own_exponent / totals).astype(jnp.bfloat16)
    combined = jnp.einsum(
        "rkgc,rckd->rkgd", probability, values, preferred_element_type=jnp.float32
    )
    combined = (
        combined
        + own_probability.astype(jnp.float32)[..., None]
        * own_value.astype(jnp.float32)[:, :, None, :]
    )
    return combined.reshape(row_count, kv_here * grouping * HD).astype(jnp.bfloat16)


def shards(
    query,
    new_key,
    new_value,
    cache_key,
    cache_value,
    lengths,
    hidden_in,
    out_weight,
    norm_gain,
    route_ids,
    route_weight,
    w_gate,
    w_up,
    w_down,
):
    heads_out = attend_local(query, new_key, new_value, cache_key, cache_value, lengths)
    n_data = lax.axis_size("dp")
    n_heads_axis = lax.axis_size("tensor")
    tok_here = hidden_in.shape[0]
    width = hidden_in.shape[1]
    partial_cols = jnp.dot(
        lax.all_gather(heads_out, "dp", axis=0, tiled=True),
        out_weight,
        preferred_element_type=jnp.float32,
    )
    by_rows = lax.all_to_all(partial_cols, "dp", split_axis=0, concat_axis=1, tiled=True)
    summed = lax.psum_scatter(by_rows, "tensor", scatter_dimension=0, tiled=True)
    attended = (hidden_in.astype(jnp.float32) + summed).astype(jnp.bfloat16)
    widened = attended.astype(jnp.float32)
    scaled = widened * lax.rsqrt(jnp.mean(widened * widened, axis=-1, keepdims=True) + 1e-06)
    normed = (scaled * norm_gain).astype(jnp.bfloat16)
    chosen_count = route_ids.shape[1]
    experts_all = n_data * n_heads_axis
    pair_count = tok_here * chosen_count
    capacity = max(2, 3 * tok_here * chosen_count // experts_all)
    flat_ids = route_ids.reshape(pair_count)
    expert_hits = (flat_ids[:, None] == jnp.arange(experts_all, dtype=jnp.int32)[None, :]).astype(
        jnp.int32
    )
    earlier = jnp.cumsum(expert_hits, axis=0) - expert_hits
    slot_index = jnp.sum(earlier * expert_hits, axis=1)
    target = flat_ids * capacity + slot_index
    placement = (
        jnp.arange(experts_all * capacity, dtype=jnp.int32)[:, None] == target[None, :]
    ).astype(jnp.bfloat16)
    token_place = jnp.sum(placement.reshape(experts_all * capacity, tok_here, chosen_count), axis=2)
    outgoing = jnp.dot(token_place, normed, preferred_element_type=jnp.float32).astype(jnp.bfloat16)
    outgoing = outgoing.reshape(experts_all, capacity, width)
    received = lax.all_to_all(outgoing, ("dp", "tensor"), split_axis=0, concat_axis=0, tiled=True)
    flat_rows = received.reshape(-1, width)
    gate_part = jnp.dot(flat_rows, w_gate[0], preferred_element_type=jnp.float32)
    up_part = jnp.dot(flat_rows, w_up[0], preferred_element_type=jnp.float32)
    activation = (jax.nn.silu(gate_part) * up_part).astype(jnp.bfloat16)
    result = jnp.dot(activation, w_down[0], preferred_element_type=jnp.float32).astype(jnp.bfloat16)
    returned = lax.all_to_all(
        result.reshape(received.shape), ("dp", "tensor"), split_axis=0, concat_axis=0, tiled=True
    )
    returned = returned.reshape(experts_all * capacity, width)
    pair_rows = jnp.einsum("sp,sd->pd", placement, returned, preferred_element_type=jnp.float32)
    weighted = route_weight[..., None] * pair_rows.reshape(tok_here, chosen_count, width)
    expert_mix = jnp.sum(weighted, axis=1).astype(jnp.bfloat16)
    return (attended, expert_mix)


def solution(mesh):
    in_specs = (
        P("dp", "tensor"),
        P("dp", "tensor"),
        P("dp", "tensor"),
        P("dp", None, "tensor"),
        P("dp", None, "tensor"),
        P("dp"),
        P(("dp", "tensor"), None),
        P("tensor", "dp"),
        P(),
        P(("dp", "tensor"), None),
        P(("dp", "tensor"), None),
        P(("dp", "tensor"), None, None),
        P(("dp", "tensor"), None, None),
        P(("dp", "tensor"), None, None),
    )
    out_specs = (P(("dp", "tensor"), None), P(("dp", "tensor"), None))
    return jax.shard_map(shards, mesh=mesh, in_specs=in_specs, out_specs=out_specs, check_vma=False)
```

profile of v0, /device:TPU:0, one launch (start us, length us, event | category | flops | bytes accessed | tf_op | source)
XLA Modules:
  0.0 355.0 jit_solution(17587841638424498671)
XLA Ops:
  7.2 0.9 iota_compare_fusion.3
  8.1 1.0 copy.35
  9.1 0.9 fusion.39
  10.1 2.4 select_reduce_fusion
  12.5 0.3 fusion.21
  12.9 0.6 fusion.17
  13.5 0.7 copy.40
  14.2 47.0 %all-gather.2.cloned.1.call-done = bf16[384,2048]{1,0:T(8,128)(2,1)} async-done(((bf16[48,2048]{1,0:T(8,128)(2,1)}), bf16[384,2048]{1,0:T(8,128)(2,1)}) %all-gather.2.cloned.1.call-update) | async-done | bytes 1572880 | tf_op jit(solution)/shard_map/all_gather | solution.py:68
  61.3 3.3 fusion.46
  64.6 3.7 %all-to-all-start = ((f32[8,48,512]{2,1,0:T(8,128)}), f32[8,48,512]{2,1,0:T(8,128)S(1)}, u32[]{:S(2)}, u32[]{:S(2)}) async-start(f32[8,48,512]{2,1,0:T(8,128)} %bitcast.50), calls=%async_computation | async-start | bytes 1572864 | tf_op jit(solution)/shard_map/all_to_all | solution.py:72
  68.4 0.1 fusion.38
  68.5 0.1 reduce_window_sum.11
  68.7 0.2 select_reduce_fusion.1
  68.9 18.8 %all-to-all-done = f32[8,48,512]{2,1,0:T(8,128)S(1)} async-done(((f32[8,48,512]{2,1,0:T(8,128)}), f32[8,48,512]{2,1,0:T(8,128)S(1)}, u32[]{:S(2)}, u32[]{:S(2)}) %all-to-all-start) | async-done | bytes 786464 | tf_op jit(solution)/shard_map/all_to_all | solution.py:72
  87.7 0.9 copy.34
  88.6 14.8 %fusion = f32[16,4096]{1,0:T(8,128)S(1)} fusion(f32[48,4096]{1,0:T(8,128)} %bitcast.47), kind=kCustom, calls=%all-reduce-scatter | all-reduce-scatter fusion | flops 262145 | bytes 1049088
  103.5 1.3 collective-permute-start
  104.8 0.6 dynamic-slice.4
  106.1 0.1 fusion.36
  106.2 0.3 concatenate
  106.6 0.2 fusion.22
  106.8 2.2 convolution_convert_fusion
  109.0 4.6 %reshape.163 = bf16[32,9,4096]{2,1,0:T(8,128)(2,1)} reshape(bf16[288,4096]{1,0:T(8,128)(2,1)} %convolution_convert_fusion) | data formatting | bytes 4718592 | tf_op jit(solution)/shard_map/reshape | solution.py:94
  113.6 102.4 %all_to_all.29 = bf16[32,9,4096]{2,1,0:T(8,128)(2,1)} all-to-all(bf16[32,9,4096]{2,1,0:T(8,128)(2,1)} %reshape.163), channel_id=1, replica_groups=mesh['dp'=8,'tensor'=4] {'dp','tensor'}, dimensions={0} | all-to-all | bytes 4718592 | tf_op jit(solution)/shard_map/all_to_all | solution.py:95
  216.0 4.7 %reshape.164 = bf16[288,4096]{1,0:T(8,128)(2,1)} reshape(bf16[32,9,4096]{2,1,0:T(8,128)(2,1)} %all_to_all.29) | data formatting | bytes 4718592 | tf_op jit(solution)/shard_map/reshape | solution.py:96
  220.7 5.5 %fusion.5 = f32[288,768]{1,0:T(8,128)S(1)} fusion(bf16[288,4096]{1,0:T(8,128)(2,1)} %reshape.164, bf16[1,4096,768]{2,1,0:T(8,128)(2,1)} %param.25), kind=kOutput, calls=%fused_computation.4 | convolution fusion | flops 1811939328 | bytes 9535488 | tf_op jit(solution)/shard_map/dot_general | solution.py:97
  226.2 11.8 %fusion.7 = bf16[288,4096]{1,0:T(8,128)(2,1)} fusion(bf16[1,768,4096]{2,1,0:T(8,128)(2,1)} %param.27, bf16[288,4096]{1,0:T(8,128)(2,1)} %reshape.164, bf16[1,4096,768]{2,1,0:T(8,128)(2,1)} %param.26, f32[288,768]{1,0:T(8,128)S(1)} %fusion.5), kind=kOutput, calls=%fused_computation.6 | convolution fusion | flops 3626385408 | bytes 18186240 | tf_op jit(solution)/shard_map/dot_general | solution.py:100
  238.0 4.6 %reshape.165 = bf16[32,9,4096]{2,1,0:T(8,128)(2,1)} reshape(bf16[288,4096]{1,0:T(8,128)(2,1)} %fusion.7) | data formatting | bytes 4718592 | tf_op jit(solution)/shard_map/reshape | solution.py:102
  242.7 3.8 %all-to-all-start.2 = ((bf16[32,9,4096]{2,1,0:T(8,128)(2,1)}), bf16[32,9,4096]{2,1,0:T(8,128)(2,1)}, u32[]{:S(2)}, u32[]{:S(2)}) async-start(bf16[32,9,4096]{2,1,0:T(8,128)(2,1)} %reshape.165), calls=%async_computation.2 | async-start | bytes 8388608 | tf_op jit(solution)/shard_map/all_to_all | solution.py:101
  246.5 93.6 %all-to-all-done.2 = bf16[32,9,4096]{2,1,0:T(8,128)(2,1)} async-done(((bf16[32,9,4096]{2,1,0:T(8,128)(2,1)}), bf16[32,9,4096]{2,1,0:T(8,128)(2,1)}, u32[]{:S(2)}, u32[]{:S(2)}) %all-to-all-start.2) | async-done | bytes 2359328 | tf_op jit(solution)/shard_map/all_to_all | solution.py:101
  340.1 4.7 %reshape.169 = bf16[288,4096,1]{1,0,2:T(8,128)(2,1)} reshape(bf16[32,9,4096]{2,1,0:T(8,128)(2,1)} %all-to-all-done.2) | data formatting | bytes 4718592 | tf_op jit(solution)/shard_map/reshape | solution.py:104
  344.8 3.3 fusion.10
  (32 shorter events, 0.5 us)
Async XLA Ops:
  7.2 54.1 %copy-start = (bf16[2048,512]{1,0:T(8,128)(2,1)S(1)}, bf16[2048,512]{1,0:T(8,128)(2,1)}, u32[]{:S(2)}) copy-start(bf16[2048,512]{1,0:T(8,128)(2,1)} %param.21) | copy-start | bytes 6291460
  7.2 5.7 %copy-start.4 = (bf16[48,128]{1,0:T(8,128)(2,1)S(1)}, bf16[48,128]{1,0:T(8,128)(2,1)}, u32[]{:S(2)}) copy-start(bf16[48,128]{1,0:T(8,128)(2,1)} %param.16) | copy-start | bytes 36868
  7.2 54.1 %all-gather.2.cloned.1.call-start = ((), (), s32[]{:S(2)}) async-start(), calls=%async_computation.3 | async-start | bytes 1769472 | tf_op jit(solution)/shard_map/all_gather | solution.py:68
  7.2 5.6 %copy-start.8 = (bf16[48,128,128]{2,1,0:T(8,128)(2,1)S(1)}, bf16[48,128,128]{2,1,0:T(8,128)(2,1)}, u32[]{:S(2)}) copy-start(bf16[48,128,128]{2,1,0:T(8,128)(2,1)} %param.18) | copy-start | bytes 4718596
  14.2 54.0 %copy-start.5 = (s32[12,8]{0,1:T(8,128)S(1)}, s32[12,8]{0,1:T(8,128)}, u32[]{:S(2)}) copy-start(s32[12,8]{0,1:T(8,128)} %param.23) | copy-start | bytes 1156
  64.6 40.3 %copy-start.7 = (u32[32]{0:T(128)S(1)}, u32[32]{0:T(128)}, u32[]{:S(2)}) copy-start(u32[32]{0:T(128)} %constant.35) | copy-start | bytes 388
  64.6 23.1 %all-to-all-start = ((f32[8,48,512]{2,1,0:T(8,128)}), f32[8,48,512]{2,1,0:T(8,128)S(1)}, u32[]{:S(2)}, u32[]{:S(2)}) async-start(f32[8,48,512]{2,1,0:T(8,128)} %bitcast.50), calls=%async_computation | async-start | bytes 1572864 | tf_op jit(solution)/shard_map/all_to_all | solution.py:72
  68.3 38.3 %copy-start.2 = (bf16[12,4096]{1,0:T(8,128)(2,1)S(1)}, bf16[12,4096]{1,0:T(8,128)(2,1)}, u32[]{:S(2)}) copy-start(bf16[12,4096]{1,0:T(8,128)(2,1)} %param.20) | copy-start | bytes 294916
  87.7 19.1 %copy-start.3 = (f32[4096]{0:T(1024)S(1)}, f32[4096]{0:T(1024)}, u32[]{:S(2)}) copy-start(f32[4096]{0:T(1024)} %param.22) | copy-start | bytes 49156
  103.5 2.7 collective-permute-start
  106.7 6.9 %copy-start.1 = (bf16[12,4096]{1,0:T(8,128)(2,1)}, bf16[12,4096]{1,0:T(8,128)(2,1)S(1)}, u32[]{:S(2)}) copy-start(bf16[12,4096]{1,0:T(8,128)(2,1)S(1)} %get-tuple-element.3) | copy-start | bytes 294916
  242.7 3.8 %copy-start.6 = (f32[12,8]{0,1:T(8,128)S(1)}, f32[12,8]{0,1:T(8,128)}, u32[]{:S(2)}) copy-start(f32[12,8]{0,1:T(8,128)} %param.24) | copy-start | bytes 1156
  242.7 97.5 %all-to-all-start.2 = ((bf16[32,9,4096]{2,1,0:T(8,128)(2,1)}), bf16[32,9,4096]{2,1,0:T(8,128)(2,1)}, u32[]{:S(2)}, u32[]{:S(2)}) async-start(bf16[32,9,4096]{2,1,0:T(8,128)(2,1)} %reshape.165), calls=%async_computation.2 | async-start | bytes 8388608 | tf_op jit(solution)/shard_map/all_to_all | solution.py:101
Sparse Core Ops, SparseCore 0:
  14.3 46.8 all-gather.1
where the time goes:
time: 356 us; the launch traced here: 355 us
  waiting for transfers between devices  159 us (45%)
  blocking collectives  117 us (33%)
  matrix products  30.1 us (8%)
  local copies, waits for them, and re-layouts  22.6 us (6%)
  between operations  14.9 us (4%)
  starting transfers between devices  8.81 us (2%)
    all_to_all x1, blocking collectives, shards(): lax.all_to_all(outgoing, ('dp', 'tensor'), split_axis=0, concat_axis=0, t...  102 us
    all_to_all x1, waiting for transfers between devices, shards(): lax.all_to_all(result.reshape(received.shape), ('dp', 'tensor'), split_ax...  93.6 us
    all_gather x1, waiting for transfers between devices, shards(): lax.all_gather(heads_out, 'dp', axis=0, tiled=True)  47 us
    all_to_all x1, waiting for transfers between devices, shards(): lax.all_to_all(partial_cols, 'dp', split_axis=0, concat_axis=1, tiled=True)  18.8 us
    unnamed x1, blocking collectives  14.8 us
    dot_general x1, matrix products, shards(): jnp.dot(activation, w_down[0], preferred_element_type=jnp.float32)  11.8 us
  transfers between devices with their start and end apart: 4, of which 3 were waited for; matrix products, arithmetic and copies ran while one was open for 0% of the time, Pallas kernels for 0%

commit v1 on v0

--- a/solution.py
+++ b/solution.py
@@ -69,7 +69,20 @@
         out_weight,
         preferred_element_type=jnp.float32,
     )
-    by_rows = lax.all_to_all(partial_cols, "dp", split_axis=0, concat_axis=1, tiled=True)
+    local_next, state_next = (jax.lax.psum(1, axis_name="dp"), jax.lax.axis_index("dp"))
+    b_next = partial_cols.shape[0] // local_next
+    front = list(partial_cols.shape)
+    front[0] = b_next
+    near = front[1]
+    front[1] = near * local_next
+    by_rows = jnp.zeros(front, partial_cols.dtype)
+    for pp in range(local_next):
+        extra = lax.dynamic_slice_in_dim(partial_cols, (state_next ^ pp) * b_next, b_next, axis=0)
+        if pp:
+            extra = jax.lax.ppermute(
+                extra, "dp", tuple(((hop_no, hop_no ^ pp) for hop_no in range(local_next)))
+            )
+        by_rows = lax.dynamic_update_slice_in_dim(by_rows, extra, (state_next ^ pp) * near, axis=1)
     summed = lax.psum_scatter(by_rows, "tensor", scatter_dimension=0, tiled=True)
     attended = (hidden_in.astype(jnp.float32) + summed).astype(jnp.bfloat16)
     widened = attended.astype(jnp.float32)

time: 356 us -> 352 us (0.989)
  waiting for transfers between devices: 159 us -> 148 us
  starting transfers between devices: 8.81 us -> 16.4 us
    all_to_all x1 -> x0, waiting for transfers between devices: 18.8 us -> none  [shards(): lax.all_to_all(partial_cols, 'dp', split_axis=0, concat_axis=1, tiled=True)]
    ppermute x0 -> x7, starting transfers between devices: none -> 11.3 us  [shards(): jax.lax.ppermute(extra, 'dp', tuple(((hop_no, hop_no ^ pp) for hop_no in...]
    ppermute x0 -> x7, waiting for transfers between devices: none -> 7.44 us  [shards(): jax.lax.ppermute(extra, 'dp', tuple(((hop_no, hop_no ^ pp) for hop_no in...]
    all_to_all x1 -> x0, starting transfers between devices: 3.68 us -> none  [shards(): lax.all_to_all(partial_cols, 'dp', split_axis=0, concat_axis=1, tiled=True)]
  transfers between devices with their start and end apart: 4 -> 10, of which waited for: 3 -> 4; matrix products, arithmetic and copies ran while one was open for 0% -> 1% of each run, Pallas kernels for 0% -> 0%
where the time goes in v1:
time: 352 us; the launch traced here: 351 us
  waiting for transfers between devices  148 us (42%)
  blocking collectives  118 us (34%)
  matrix products  29.2 us (8%)
  local copies, waits for them, and re-layouts  23.5 us (7%)
  starting transfers between devices  16.4 us (5%)
  between operations  15.1 us (4%)
    all_to_all x1, blocking collectives, shards(): lax.all_to_all(outgoing, ('dp', 'tensor'), split_axis=0, concat_axis=0, t...  103 us
    all_to_all x1, waiting for transfers between devices, shards(): lax.all_to_all(result.reshape(received.shape), ('dp', 'tensor'), split_ax...  93.6 us
    all_gather x1, waiting for transfers between devices, shards(): lax.all_gather(heads_out, 'dp', axis=0, tiled=True)  46.6 us
    unnamed x1, blocking collectives  14.3 us
    dot_general x1, matrix products, shards(): jnp.dot(activation, w_down[0], preferred_element_type=jnp.float32)  11.8 us
    ppermute x7, starting transfers between devices, shards(): jax.lax.ppermute(extra, 'dp', tuple(((hop_no, hop_no ^ pp) for hop_no in...  11.3 us
    ppermute x7, waiting for transfers between devices, shards(): jax.lax.ppermute(extra, 'dp', tuple(((hop_no, hop_no ^ pp) for hop_no in...  7.44 us
  transfers between devices with their start and end apart: 10, of which 4 were waited for; matrix products, arithmetic and copies ran while one was open for 1% of the time, Pallas kernels for 0%

profile of v1, /device:TPU:0, one launch (start us, length us, event | category | flops | bytes accessed | tf_op | source)
XLA Modules:
  0.0 351.3 jit_solution(13287293192389831828)
XLA Ops:
  7.2 0.9 iota_compare_fusion.3
  8.1 1.0 copy.30
  9.1 0.9 fusion.39
  10.1 2.4 select_reduce_fusion
  12.9 0.6 fusion.17
  13.5 0.7 copy.35
  14.8 46.6 %all-gather.2.cloned.1.call-done = bf16[384,2048]{1,0:T(8,128)(2,1)} async-done(((bf16[48,2048]{1,0:T(8,128)(2,1)}), bf16[384,2048]{1,0:T(8,128)(2,1)}) %all-gather.2.cloned.1.call-update) | async-done | bytes 1572880 | tf_op jit(solution)/shard_map/all_gather | solution.py:68
  61.3 2.4 fusion.46
  63.8 0.8 constant_dynamic-slice_fusion
  65.3 1.5 collective-permute-start.1
  66.8 1.5 collective-permute-start.2
  68.3 1.7 collective-permute-start.3
  70.0 1.2 collective-permute-start.4
  71.3 1.7 collective-permute-start.5
  72.9 0.9 constant_dynamic-update-slice_fusion.6
  73.8 3.1 collective-permute-start.6
  77.0 5.4 %collective-permute-done.3 = f32[48,512]{1,0:T(8,128)S(1)} collective-permute-done((f32[48,512]{1,0:T(8,128)S(1)}, f32[48,512]{1,0:T(8,128)S(1)}, u32[]{:S(2)}, u32[]{:S(2)}) %collective-permute-start.3) | collective-permute-done | bytes 98336 | tf_op jit(solution)/shard_map/ppermute | solution.py:82
  82.4 2.1 collective-permute-done.4
  84.5 14.3 %fusion = f32[16,4096]{1,0:T(8,128)S(1)} fusion(f32[48,4096]{1,0:T(8,128)S(1)} %constant_dynamic-update-slice_fusion), kind=kCustom, calls=%all-reduce-scatter | all-reduce-scatter fusion | flops 262145 | bytes 1049088
  98.9 1.3 collective-permute-start.7
  100.2 0.6 dynamic-slice.4
  102.1 2.3 convolution_convert_fusion
  104.4 4.6 %reshape.160 = bf16[32,9,4096]{2,1,0:T(8,128)(2,1)} reshape(bf16[288,4096]{1,0:T(8,128)(2,1)} %convolution_convert_fusion) | data formatting | bytes 4718592 | tf_op jit(solution)/shard_map/reshape | solution.py:107
  109.0 103.3 %all_to_all.10 = bf16[32,9,4096]{2,1,0:T(8,128)(2,1)} all-to-all(bf16[32,9,4096]{2,1,0:T(8,128)(2,1)} %reshape.160), channel_id=1, replica_groups=mesh['dp'=8,'tensor'=4] {'dp','tensor'}, dimensions={0} | all-to-all | bytes 4718592 | tf_op jit(solution)/shard_map/all_to_all | solution.py:108
  212.3 4.7 %reshape.161 = bf16[288,4096]{1,0:T(8,128)(2,1)} reshape(bf16[32,9,4096]{2,1,0:T(8,128)(2,1)} %all_to_all.10) | data formatting | bytes 4718592 | tf_op jit(solution)/shard_map/reshape | solution.py:109
  217.0 5.5 %fusion.5 = f32[288,768]{1,0:T(8,128)S(1)} fusion(bf16[288,4096]{1,0:T(8,128)(2,1)} %reshape.161, bf16[1,4096,768]{2,1,0:T(8,128)(2,1)} %param.25), kind=kOutput, calls=%fused_computation.4 | convolution fusion | flops 1811939328 | bytes 9535488 | tf_op jit(solution)/shard_map/dot_general | solution.py:110
  222.5 11.8 %fusion.7 = bf16[288,4096]{1,0:T(8,128)(2,1)} fusion(bf16[1,768,4096]{2,1,0:T(8,128)(2,1)} %param.27, bf16[288,4096]{1,0:T(8,128)(2,1)} %reshape.161, bf16[1,4096,768]{2,1,0:T(8,128)(2,1)} %param.26, f32[288,768]{1,0:T(8,128)S(1)} %fusion.5), kind=kOutput, calls=%fused_computation.6 | convolution fusion | flops 3626385408 | bytes 18186240 | tf_op jit(solution)/shard_map/dot_general | solution.py:113
  234.4 4.6 %reshape.162 = bf16[32,9,4096]{2,1,0:T(8,128)(2,1)} reshape(bf16[288,4096]{1,0:T(8,128)(2,1)} %fusion.7) | data formatting | bytes 4718592 | tf_op jit(solution)/shard_map/reshape | solution.py:115
  239.0 3.8 %all-to-all-start.1 = ((bf16[32,9,4096]{2,1,0:T(8,128)(2,1)}), bf16[32,9,4096]{2,1,0:T(8,128)(2,1)}, u32[]{:S(2)}, u32[]{:S(2)}) async-start(bf16[32,9,4096]{2,1,0:T(8,128)(2,1)} %reshape.162), calls=%async_computation.1 | async-start | bytes 8388608 | tf_op jit(solution)/shard_map/all_to_all | solution.py:114
  242.9 93.6 %all-to-all-done.1 = bf16[32,9,4096]{2,1,0:T(8,128)(2,1)} async-done(((bf16[32,9,4096]{2,1,0:T(8,128)(2,1)}), bf16[32,9,4096]{2,1,0:T(8,128)(2,1)}, u32[]{:S(2)}, u32[]{:S(2)}) %all-to-all-start.1) | async-done | bytes 2359328 | tf_op jit(solution)/shard_map/all_to_all | solution.py:114
  336.5 4.7 %reshape.166 = bf16[288,4096,1]{1,0,2:T(8,128)(2,1)} reshape(bf16[32,9,4096]{2,1,0:T(8,128)(2,1)} %all-to-all-done.1) | data formatting | bytes 4718592 | tf_op jit(solution)/shard_map/reshape | solution.py:117
  341.2 3.3 fusion.10
  (52 shorter events, 2.5 us)
Async XLA Ops:
  7.2 54.1 %copy-start = (bf16[2048,512]{1,0:T(8,128)(2,1)S(1)}, bf16[2048,512]{1,0:T(8,128)(2,1)}, u32[]{:S(2)}) copy-start(bf16[2048,512]{1,0:T(8,128)(2,1)} %param.21) | copy-start | bytes 6291460
  7.2 5.7 %copy-start.4 = (bf16[48,128]{1,0:T(8,128)(2,1)S(1)}, bf16[48,128]{1,0:T(8,128)(2,1)}, u32[]{:S(2)}) copy-start(bf16[48,128]{1,0:T(8,128)(2,1)} %param.16) | copy-start | bytes 36868
  7.2 54.1 %all-gather.2.cloned.1.call-start = ((), (), s32[]{:S(2)}) async-start(), calls=%async_computation.2 | async-start | bytes 1769472 | tf_op jit(solution)/shard_map/all_gather | solution.py:68
  7.2 5.6 %copy-start.8 = (bf16[48,128,128]{2,1,0:T(8,128)(2,1)S(1)}, bf16[48,128,128]{2,1,0:T(8,128)(2,1)}, u32[]{:S(2)}) copy-start(bf16[48,128,128]{2,1,0:T(8,128)(2,1)} %param.18) | copy-start | bytes 4718596
  12.5 1.8 copy-start.5
  63.8 36.4 %copy-start.7 = (u32[32]{0:T(128)S(1)}, u32[32]{0:T(128)}, u32[]{:S(2)}) copy-start(u32[32]{0:T(128)} %constant.64) | copy-start | bytes 388
  64.5 37.4 %copy-start.2 = (bf16[12,4096]{1,0:T(8,128)(2,1)S(1)}, bf16[12,4096]{1,0:T(8,128)(2,1)}, u32[]{:S(2)}) copy-start(bf16[12,4096]{1,0:T(8,128)(2,1)} %param.20) | copy-start | bytes 294916
  64.5 37.6 %copy-start.3 = (f32[4096]{0:T(1024)S(1)}, f32[4096]{0:T(1024)}, u32[]{:S(2)}) copy-start(f32[4096]{0:T(1024)} %param.22) | copy-start | bytes 49156
  64.5 6.7 %collective-permute-start = (f32[48,512]{1,0:T(8,128)}, f32[48,512]{1,0:T(8,128)}, u32[]{:S(2)}, u32[]{:S(2)}) collective-permute-start(f32[48,512]{1,0:T(8,128)} %get-tuple-element.10), channel_id=1, source_target_pairs={{0,4},{4,0},{8,12},{12,8},{16,20},{20,16},{24,28},{28,24},{1,5},{5... | collective-permute-start | bytes 294920 | tf_op jit(solution)/shard_map/ppermute | solution.py:82
  65.3 8.5 %collective-permute-start.1 = (f32[48,512]{1,0:T(8,128)}, f32[48,512]{1,0:T(8,128)S(1)}, u32[]{:S(2)}, u32[]{:S(2)}) collective-permute-start(f32[48,512]{1,0:T(8,128)} %get-tuple-element.9), channel_id=1, source_target_pairs={{0,8},{4,12},{8,0},{12,4},{16,24},{20,28},{24,16},{28,20},{1,9},{5... | collective-permute-start | bytes 294920 | tf_op jit(solution)/shard_map/ppermute | solution.py:82
  66.8 10.1 %collective-permute-start.2 = (f32[48,512]{1,0:T(8,128)}, f32[48,512]{1,0:T(8,128)S(1)}, u32[]{:S(2)}, u32[]{:S(2)}) collective-permute-start(f32[48,512]{1,0:T(8,128)} %get-tuple-element.8), channel_id=1, source_target_pairs={{0,12},{4,8},{8,4},{12,0},{16,28},{20,24},{24,20},{28,16},{1,13},{... | collective-permute-start | bytes 294920 | tf_op jit(solution)/shard_map/ppermute | solution.py:82
  68.3 14.0 %collective-permute-start.3 = (f32[48,512]{1,0:T(8,128)S(1)}, f32[48,512]{1,0:T(8,128)S(1)}, u32[]{:S(2)}, u32[]{:S(2)}) collective-permute-start(f32[48,512]{1,0:T(8,128)S(1)} %get-tuple-element.7), channel_id=1, source_target_pairs={{0,16},{4,20},{8,24},{12,28},{16,0},{20,4},{24,8},{28,12},{1,17},{... | collective-permute-start | bytes 294920 | tf_op jit(solution)/shard_map/ppermute | solution.py:82
  70.0 14.4 %collective-permute-start.4 = (f32[48,512]{1,0:T(8,128)S(1)}, f32[48,512]{1,0:T(8,128)S(1)}, u32[]{:S(2)}, u32[]{:S(2)}) collective-permute-start(f32[48,512]{1,0:T(8,128)S(1)} %get-tuple-element.6), channel_id=1, source_target_pairs={{0,20},{4,16},{8,28},{12,24},{16,4},{20,0},{24,12},{28,8},{1,21},{... | collective-permute-start | bytes 294920 | tf_op jit(solution)/shard_map/ppermute | solution.py:82
  71.3 13.2 %collective-permute-start.5 = (f32[48,512]{1,0:T(8,128)S(1)}, f32[48,512]{1,0:T(8,128)S(1)}, u32[]{:S(2)}, u32[]{:S(2)}) collective-permute-start(f32[48,512]{1,0:T(8,128)S(1)} %get-tuple-element.5), channel_id=1, source_target_pairs={{0,24},{4,28},{8,16},{12,20},{16,8},{20,12},{24,0},{28,4},{1,25},{... | collective-permute-start | bytes 294920 | tf_op jit(solution)/shard_map/ppermute | solution.py:82
  73.8 10.7 %collective-permute-start.6 = (f32[48,512]{1,0:T(8,128)S(1)}, f32[48,512]{1,0:T(8,128)S(1)}, u32[]{:S(2)}, u32[]{:S(2)}) collective-permute-start(f32[48,512]{1,0:T(8,128)S(1)} %get-tuple-element.4), channel_id=1, source_target_pairs={{0,28},{4,24},{8,20},{12,16},{16,12},{20,8},{24,4},{28,0},{1,29},{... | collective-permute-start | bytes 294920 | tf_op jit(solution)/shard_map/ppermute | solution.py:82
  98.9 2.7 collective-permute-start.7
  102.1 6.9 %copy-start.1 = (bf16[12,4096]{1,0:T(8,128)(2,1)}, bf16[12,4096]{1,0:T(8,128)(2,1)S(1)}, u32[]{:S(2)}) copy-start(bf16[12,4096]{1,0:T(8,128)(2,1)S(1)} %get-tuple-element.3) | copy-start | bytes 294916
  239.0 3.8 %copy-start.6 = (f32[12,8]{0,1:T(8,128)S(1)}, f32[12,8]{0,1:T(8,128)}, u32[]{:S(2)}) copy-start(f32[12,8]{0,1:T(8,128)} %param.24) | copy-start | bytes 1156
  239.0 97.5 %all-to-all-start.1 = ((bf16[32,9,4096]{2,1,0:T(8,128)(2,1)}), bf16[32,9,4096]{2,1,0:T(8,128)(2,1)}, u32[]{:S(2)}, u32[]{:S(2)}) async-start(bf16[32,9,4096]{2,1,0:T(8,128)(2,1)} %reshape.162), calls=%async_computation.1 | async-start | bytes 8388608 | tf_op jit(solution)/shard_map/all_to_all | solution.py:114
Sparse Core Ops, SparseCore 0:
  14.4 46.8 all-gather.1
